TPU v7x, 256 devices: a whole 4x4x8 slice. The times are simulated.
256 devices in a mesh: dp: 16 (over x, y), expert: 16 (over z, core).
Axes of the slice: x: 4, y: 4, z: 8, core: 2. Of those that a mesh axis runs over, the one named last changes fastest.
Arguments:
- hidden: bfloat16 [32768, 8, 768], P(('dp', 'expert')), may hold values from -6 to 6
- upstream: bfloat16 [32768, 4096], P(('dp', 'expert')), may hold values from -0.125 to 0.125
- probs: bfloat16 [32768, 8], P(('dp', 'expert')), may hold values from 0.019897461 to 0.5
- expert_ids: int32 [32768, 8], P(('dp', 'expert')), may hold values from 0 to 15, all different within a row; in each aligned block of 128 rows (0 to 127, 128 to 255, ...) at most 72 rows name the same one
- w_down: bfloat16 [16, 4096, 768], P('expert', 'dp'), may hold values from -0.21875 to 0.21875
Outputs:
- grad_down: float32 [16, 4096, 768], P('expert', 'dp')
- gate_grad: float32 [32768, 8], P(('dp', 'expert'))
Inputs may be any that keep to these rules, and one draw needn't show every extreme that they name: `expert_ids`: each row names 8 different experts; among the rows of one device no expert is named by more than 72 rows, a bound that some block reaches.
All inputs are finite; a program needn't handle non-finite values.
Results may differ from a plain program's by a relative error of at most 0.013.
Values may be sent and summed in bfloat16 or wider, within the bound.
No kernel may reach another device: no remote copies, remote signals or barrier semaphores. Data moves between devices by JAX's collectives and lax.ppermute only.
A program may use at most 128 MiB of HBM per device.

v0:
```python
import jax
import jax.numpy as jnp
from jax import lax
from jax.sharding import Mesh, PartitionSpec as P


def body(hidden, upstream, probs, expert_ids, w_down):
    tok_rows, top_k = expert_ids.shape
    hid_width = hidden.shape[2]
    model_width = upstream.shape[1]
    lanes = 128
    n_z = lax.axis_size("z")
    n_core = lax.axis_size("core")
    groups = n_z * n_core
    n_dp = lax.axis_size("dp")
    slots_per = max(tok_rows * 9 // 16, tok_rows * top_k // groups)
    total_rows = groups * slots_per
    chosen = (expert_ids[:, :, None] == jnp.arange(groups, dtype=jnp.int32)[None, None, :]).astype(
        jnp.int32
    )
    member = jnp.sum(chosen, axis=1)
    slot_place = jnp.cumsum(member, axis=0) - 1
    which_k = jnp.sum(chosen * jnp.arange(top_k, dtype=jnp.int32)[None, :, None], axis=1)
    target = (
        (member == 1)[:, :, None]
        & (slot_place[:, :, None] == jnp.arange(slots_per, dtype=jnp.int32)[None, None, :])
    ).astype(jnp.int32)
    filled = jnp.sum(target, axis=0) == 1
    source_tok = jnp.sum(target * jnp.arange(tok_rows, dtype=jnp.int32)[:, None, None], axis=0)
    source_k = jnp.sum(target * which_k[:, :, None], axis=0)
    flat_index = (source_tok * top_k + source_k).reshape(-1)
    picked_h = hidden.reshape(tok_rows * top_k, hid_width)[flat_index].reshape(
        groups, slots_per, hid_width
    )
    send_h = jnp.where(filled[:, :, None], picked_h, jnp.zeros_like(picked_h))
    picked_p = probs.reshape(-1)[flat_index].reshape(groups, slots_per)
    send_p = jnp.where(filled, picked_p, jnp.zeros_like(picked_p))
    dy3 = upstream.reshape(tok_rows, model_width // lanes, lanes)
    dy_z = lax.all_gather(dy3, "z", axis=0, tiled=True)
    dy_pair = lax.ppermute(dy_z, "core", perm=[(c, (c + 1) % n_core) for c in range(n_core)])
    dy_all = jnp.concatenate([dy_z, dy_pair], axis=0)
    w_blocks = lax.all_to_all(
        jnp.broadcast_to(w_down, (n_dp,) + w_down.shape[1:]),
        "dp",
        split_axis=0,
        concat_axis=0,
        tiled=True,
    )
    w_full = w_blocks.reshape(n_dp * w_down.shape[1] // lanes, lanes, hid_width)
    ez = ("z", "core")
    recv_h, recv_p, recv_tok = (
        lax.all_to_all(send_h, ez, split_axis=0, concat_axis=0, tiled=True),
        lax.all_to_all(send_p, ez, split_axis=0, concat_axis=0, tiled=True),
        lax.all_to_all(source_tok, ez, split_axis=0, concat_axis=0, tiled=True),
    )
    src = jnp.arange(groups, dtype=jnp.int32)
    src_z, src_core = (src // n_core, src % n_core)
    my_core = lax.axis_index("core")
    block = (src_core - my_core + n_core) % n_core
    row_of = recv_tok + (tok_rows * (block * n_z + src_z))[:, None]
    rows_h = recv_h.reshape(total_rows, hid_width)
    rows_dy = dy_all[row_of.reshape(-1)]
    projected = lax.dot_general(
        rows_h, w_full, (((1,), (2,)), ((), ())), preferred_element_type=jnp.float32
    )
    scores = jnp.sum(projected * rows_dy.astype(jnp.float32), axis=(1, 2))
    returned = lax.all_to_all(
        scores.reshape(groups, slots_per), ez, split_axis=0, concat_axis=0, tiled=True
    )
    scaled = (
        recv_p.reshape(total_rows, 1, 1).astype(jnp.float32) * rows_dy.astype(jnp.float32)
    ).astype(jnp.bfloat16)
    partial = lax.dot_general(
        scaled, rows_h, (((0,), (0,)), ((), ())), preferred_element_type=jnp.float32
    ).astype(jnp.bfloat16)
    grad_block = lax.psum_scatter(
        partial.reshape(model_width, hid_width), "dp", scatter_dimension=0, tiled=True
    ).astype(jnp.float32)
    place_slot = jnp.take_along_axis(slot_place, expert_ids, axis=1)
    gate_grad = returned[expert_ids, place_slot]
    return (grad_block[None], gate_grad)


def solution(mesh):
    n_dp, n_expert = mesh.devices.shape
    sub = Mesh(mesh.devices.reshape(n_dp, n_expert // 2, 2), ("dp", "z", "core"))
    tok = ("dp", "z", "core")
    in_specs = (
        P(tok, None, None),
        P(tok, None),
        P(tok, None),
        P(tok, None),
        P(("z", "core"), "dp", None),
    )
    out_specs = (P(("z", "core"), "dp", None), P(tok, None))
    return jax.shard_map(body, mesh=sub, in_specs=in_specs, out_specs=out_specs, check_vma=False)
```

profile of v0, /device:TPU:1, one launch (start us, length us, event | category | flops | bytes accessed | tf_op | source)
XLA Modules:
  0.0 389.1 jit_solution(15925728178710582814)
XLA Ops:
  7.2 2.6 copy.58
  9.8 98.1 %all-gather.2.cloned.1.call-done = bf16[1024,32,128]{2,1,0:T(8,128)(2,1)} async-done(((bf16[128,32,128]{2,1,0:T(8,128)(2,1)}), bf16[1024,32,128]{2,1,0:T(8,128)(2,1)}) %all-gather.2.cloned.1.call-update) | async-done | bytes 8388624 | tf_op jit(solution)/shard_map/all_gather | solution.py:39
  109.6 1.5 convert_reduce_fusion
  112.9 7.3 %gather_fusion = bf16[1152]{0:T(1024)(128)(2,1)S(1)} fusion(bf16[1024]{0:T(1024)(128)(2,1)S(1)} %reshape.188, s32[2048]{0:T(1024)S(1)} %pad_clamp_fusion.1), kind=kCustom, calls=%fused_computation | custom fusion | bytes 9216 | tf_op jit(solution)/shard_map/gather | solution.py:36
  120.9 4.4 %all-to-all-start = ((bf16[16,1,72]{2,1,0:T(2,128)(2,1)}), bf16[16,1,72]{2,1,0:T(2,128)(2,1)S(1)}, u32[]{:S(2)}, u32[]{:S(2)}) async-start(bf16[16,1,72]{2,1,0:T(2,128)(2,1)} %copy.51), calls=%async_computation | async-start | bytes 16384 | tf_op jit(solution)/shard_map/all_to_all | solution.py:53
  125.3 4.6 %gather_fusion.2 = bf16[1152,768]{1,0:T(8,128)(2,1)S(1)} fusion(bf16[1024,768]{1,0:T(8,128)(2,1)S(1)} %bitcast.26, s32[2048]{0:T(1024)S(1)} %pad_clamp_fusion.1), kind=kCustom, calls=%fused_computation.2 | custom fusion | bytes 3543552 | tf_op jit(solution)/shard_map/gather | solution.py:32
  129.9 2.5 all-to-all-done
  132.3 4.8 %all-to-all-start.1 = ((s32[16,1,72]{2,1,0:T(1,128)}), s32[16,1,72]{2,1,0:T(1,128)S(1)}, u32[]{:S(2)}, u32[]{:S(2)}) async-start(s32[16,1,72]{2,1,0:T(1,128)} %bitcast.2), calls=%async_computation.1 | async-start | bytes 16384 | tf_op jit(solution)/shard_map/all_to_all | solution.py:54
  138.6 5.5 %all-to-all-done.1 = s32[16,1,72]{2,1,0:T(1,128)S(1)} async-done(((s32[16,1,72]{2,1,0:T(1,128)}), s32[16,1,72]{2,1,0:T(1,128)S(1)}, u32[]{:S(2)}, u32[]{:S(2)}) %all-to-all-start.1) | async-done | bytes 4640 | tf_op jit(solution)/shard_map/all_to_all | solution.py:54
  144.1 4.2 %all-to-all-start.2 = ((bf16[16,72,768]{2,1,0:T(8,128)(2,1)}), bf16[16,72,768]{2,1,0:T(8,128)(2,1)S(1)}, u32[]{:S(2)}, u32[]{:S(2)}) async-start(bf16[16,72,768]{2,1,0:T(8,128)(2,1)} %broadcast_select_fusion), calls=%async_computation.2 | async-start | bytes 3538944 | tf_op jit(solution)/shard_map/all_to_all | solution.py:52
  149.9 16.7 %pad_maximum_fusion = bf16[2048,32,128]{2,1,0:T(8,128)(2,1)} fusion(bf16[1024,32,128]{2,1,0:T(8,128)(2,1)} %collective-permute-done, bf16[1024,32,128]{2,1,0:T(8,128)(2,1)} %all-gather.2.cloned.1.call-done), kind=kLoop, calls=%fused_computation.8 | loop fusion | flops 8388608 | bytes 33554432 | tf_op jit(solution)/shard_map/concatenate | solution.py:41
  166.6 11.8 %gather_fusion.1 = bf16[1152,32,128]{2,1,0:T(8,128)(2,1)} fusion(bf16[2048,32,128]{2,1,0:T(8,128)(2,1)} %pad_maximum_fusion, s32[2048]{0:T(1024)S(1)} %pad_clamp_fusion), kind=kCustom, calls=%fused_computation.1 | custom fusion | bytes 18878976 | tf_op jit(solution)/shard_map/gather | solution.py:62
  178.4 12.9 %copy.53 = bf16[1152,32,128]{0,2,1:T(8,128)(2,1)} copy(bf16[1152,32,128]{2,1,0:T(8,128)(2,1)} %gather_fusion.1) | data formatting | bytes 18874368 | tf_op jit(solution)/shard_map/gather | solution.py:62
  191.3 14.0 %fusion.5 = bf16[32,128,768]{2,1,0:T(8,128)(2,1)} fusion(bf16[1152,768,1]{1,0,2:T(8,128)(2,1)S(1)} %bitcast.31, bf16[1152,32,128]{0,2,1:T(8,128)(2,1)} %copy.53, f32[1152]{0:T(1024)S(1)} %reshape.196), kind=kOutput, calls=%fused_computation.12 | convolution fusion | flops 7265058816 | bytes 17502720 | tf_op jit(solution)/shard_map/dot_general | solution.py:73
  205.4 3.3 broadcast_in_dim.54
  208.7 6.6 %all-to-all-start.3 = ((bf16[16,256,768]{2,1,0:T(8,128)(2,1)}), bf16[16,256,768]{2,1,0:T(8,128)(2,1)}, u32[]{:S(2)}, u32[]{:S(2)}) async-start(bf16[16,256,768]{2,1,0:T(8,128)(2,1)} %broadcast_in_dim.54), calls=%async_computation.4 | async-start | bytes 12582912 | tf_op jit(solution)/shard_map/all_to_all | solution.py:42
  215.5 7.1 %gather_fusion.4 = s32[1024]{0:T(1024)S(1)} fusion(s32[128,16]{1,0:T(8,128)S(1)} %broadcast_add_fusion, s32[1024]{0:T(1024)S(1)} %reshape.228), kind=kCustom, calls=%fused_computation.4 | custom fusion | bytes 16384 | tf_op jit(solution)/shard_map/jit(take_along_axis)/gather | solution.py:79
  222.7 107.3 %all-to-all-done.3 = bf16[16,256,768]{2,1,0:T(8,128)(2,1)} async-done(((bf16[16,256,768]{2,1,0:T(8,128)(2,1)}), bf16[16,256,768]{2,1,0:T(8,128)(2,1)}, u32[]{:S(2)}, u32[]{:S(2)}) %all-to-all-start.3) | async-done | bytes 6291488 | tf_op jit(solution)/shard_map/all_to_all | solution.py:42
  330.0 14.2 %fusion.4 = f32[1152]{0:T(1024)S(1)} fusion(bf16[1152,32,128]{0,2,1:T(8,128)(2,1)} %copy.53, bf16[1152,768,1]{1,0,2:T(8,128)(2,1)S(1)} %bitcast.32, bf16[32,128,768]{2,1,0:T(8,128)(2,1)} %bitcast.11), kind=kOutput, calls=%fused_computation.11 | convolution fusion | flops 7261912064 | bytes 17502720 | tf_op jit(solution)/shard_map/dot_general | solution.py:63
  344.9 7.1 %all-to-all-start.4 = ((f32[16,1,72]{2,1,0:T(1,128)}), f32[16,1,72]{2,1,0:T(1,128)S(1)}, u32[]{:S(2)}, u32[]{:S(2)}) async-start(f32[16,1,72]{2,1,0:T(1,128)} %all_to_all.32), calls=%async_computation.5 | async-start | bytes 16384 | tf_op jit(solution)/shard_map/all_to_all | solution.py:67
  352.2 6.7 %all-to-all-done.4 = f32[16,1,72]{2,1,0:T(1,128)S(1)} async-done(((f32[16,1,72]{2,1,0:T(1,128)}), f32[16,1,72]{2,1,0:T(1,128)S(1)}, u32[]{:S(2)}, u32[]{:S(2)}) %all-to-all-start.4) | async-done | bytes 4640 | tf_op jit(solution)/shard_map/all_to_all | solution.py:67
  358.9 6.8 %gather_fusion.3 = f32[1024]{0:T(1024)S(1)} fusion(f32[16,72]{1,0:T(8,128)S(1)} %bitcast.27, s32[1024]{0:T(1024)S(1)} %reshape.222), kind=kCustom, calls=%fused_computation.3 | custom fusion | bytes 16384 | tf_op jit(solution)/shard_map/gather | solution.py:80
  366.4 13.9 %reduce-scatter.2.cloned.1.call-done = bf16[256,768]{1,0:T(8,128)(2,1)} async-done(((bf16[4096,768]{1,0:T(8,128)(2,1)}), bf16[256,768]{1,0:T(8,128)(2,1)}) %reduce-scatter.2.cloned.1.call-update) | async-done | bytes 393232 | tf_op jit(solution)/shard_map/reduce_scatter | solution.py:76
  380.4 1.9 bitcast_convert_fusion
  (52 shorter events, 9.3 us)
Async XLA Ops:
  7.2 118.2 %copy-start = (bf16[128,8,768]{2,1,0:T(8,128)(2,1)S(1)}, bf16[128,8,768]{2,1,0:T(8,128)(2,1)}, u32[]{:S(2)}) copy-start(bf16[128,8,768]{2,1,0:T(8,128)(2,1)} %param.5) | copy-start | bytes 4718596
  7.2 100.7 %all-gather.2.cloned.1.call-start = ((), (), s32[]{:S(2)}) async-start(), calls=%async_computation.6 | async-start | bytes 9437184 | tf_op jit(solution)/shard_map/all_gather | solution.py:39
  107.9 42.0 %collective-permute-start = (bf16[1024,32,128]{2,1,0:T(8,128)(2,1)}, bf16[1024,32,128]{2,1,0:T(8,128)(2,1)}, u32[]{:S(2)}, u32[]{:S(2)}) collective-permute-start(bf16[1024,32,128]{2,1,0:T(8,128)(2,1)} %all-gather.2.cloned.1.call-done), channel_id=1, source_target_pairs={{0,1},{1,0},{2,3},{3,2},{4,5},{5,4},{6,7},{7,6},{8,9},{9,8},{10,11... | collective-permute-start | bytes 25165832 | tf_op jit(solution)/shard_map/ppermute | solution.py:40
  120.9 11.5 %all-to-all-start = ((bf16[16,1,72]{2,1,0:T(2,128)(2,1)}), bf16[16,1,72]{2,1,0:T(2,128)(2,1)S(1)}, u32[]{:S(2)}, u32[]{:S(2)}) async-start(bf16[16,1,72]{2,1,0:T(2,128)(2,1)} %copy.51), calls=%async_computation | async-start | bytes 16384 | tf_op jit(solution)/shard_map/all_to_all | solution.py:53
  132.3 11.7 %all-to-all-start.1 = ((s32[16,1,72]{2,1,0:T(1,128)}), s32[16,1,72]{2,1,0:T(1,128)S(1)}, u32[]{:S(2)}, u32[]{:S(2)}) async-start(s32[16,1,72]{2,1,0:T(1,128)} %bitcast.2), calls=%async_computation.1 | async-start | bytes 16384 | tf_op jit(solution)/shard_map/all_to_all | solution.py:54
  144.1 47.3 %all-to-all-start.2 = ((bf16[16,72,768]{2,1,0:T(8,128)(2,1)}), bf16[16,72,768]{2,1,0:T(8,128)(2,1)S(1)}, u32[]{:S(2)}, u32[]{:S(2)}) async-start(bf16[16,72,768]{2,1,0:T(8,128)(2,1)} %broadcast_select_fusion), calls=%async_computation.2 | async-start | bytes 3538944 | tf_op jit(solution)/shard_map/all_to_all | solution.py:52
  148.2 232.1 %reduce-scatter.2.cloned.1.call-start = ((), (), s32[]{:S(2)}) async-start(), calls=%async_computation.7 | async-start | bytes 6684672 | tf_op jit(solution)/shard_map/reduce_scatter | solution.py:76
  191.3 14.0 %copy-start.2 = (bf16[1,256,768]{2,1,0:T(8,128)(2,1)S(1)}, bf16[1,256,768]{2,1,0:T(8,128)(2,1)}, u32[]{:S(2)}) copy-start(bf16[1,256,768]{2,1,0:T(8,128)(2,1)} %param.9) | copy-start | bytes 1179652
  205.3 9.9 %copy-start.3 = (s32[128,8]{0,1:T(8,128)S(1)}, s32[128,8]{0,1:T(8,128)}, u32[]{:S(2)}) copy-start(s32[128,8]{0,1:T(8,128)} %param.8) | copy-start | bytes 12292
  208.7 121.3 %all-to-all-start.3 = ((bf16[16,256,768]{2,1,0:T(8,128)(2,1)}), bf16[16,256,768]{2,1,0:T(8,128)(2,1)}, u32[]{:S(2)}, u32[]{:S(2)}) async-start(bf16[16,256,768]{2,1,0:T(8,128)(2,1)} %broadcast_in_dim.54), calls=%async_computation.4 | async-start | bytes 12582912 | tf_op jit(solution)/shard_map/all_to_all | solution.py:42
  344.9 14.0 %all-to-all-start.4 = ((f32[16,1,72]{2,1,0:T(1,128)}), f32[16,1,72]{2,1,0:T(1,128)S(1)}, u32[]{:S(2)}, u32[]{:S(2)}) async-start(f32[16,1,72]{2,1,0:T(1,128)} %all_to_all.32), calls=%async_computation.5 | async-start | bytes 16384 | tf_op jit(solution)/shard_map/all_to_all | solution.py:67
  358.9 23.4 %copy-start.1 = (bf16[128,8,768]{2,1,0:T(8,128)(2,1)S(1)}, bf16[128,8,768]{2,1,0:T(8,128)(2,1)}, u32[]{:S(2)}) copy-start(bf16[128,8,768]{2,1,0:T(8,128)(2,1)} %param.5) | copy-start | bytes 4718596
Sparse Core Ops, SparseCore 0:
  9.9 97.9 all-gather.1
  205.5 174.8 reduce-scatter.1
where the time goes:
time: 390 us; the launch traced here: 389 us
  waiting for transfers between devices  234 us (60%)
  local copies, waits for them, and re-layouts  60.9 us (16%)
  matrix products  28.2 us (7%)
  starting transfers between devices  27.8 us (7%)
  other arithmetic  24 us (6%)
  between operations  14.2 us (4%)
    all_to_all x1, waiting for transfers between devices, body(): lax.all_to_all(jnp.broadcast_to(w_down, (n_dp,) + w_down.shape[1:]), 'dp'...  107 us
    all_gather x1, waiting for transfers between devices, body(): dy_z = lax.all_gather(dy3, 'z', axis=0, tiled=True)  98.1 us
    gather x2, local copies, waits for them, and re-layouts, body(): rows_dy = dy_all[row_of.reshape(-1)]  24.7 us
    concatenate x1, other arithmetic, body(): dy_all = jnp.concatenate([dy_z, dy_pair], axis=0)  16.7 us
    dot_general x1, matrix products, body(): lax.dot_general(rows_h, w_full, (((1,), (2,)), ((), ())), preferred_eleme...  14.2 us
    dot_general x1, matrix products, body(): lax.dot_general(scaled, rows_h, (((0,), (0,)), ((), ())), preferred_eleme...  14 us
    reduce_scatter x1, waiting for transfers between devices, body(): lax.psum_scatter(partial.reshape(model_width, hid_width), 'dp', scatter_d...  13.9 us
  transfers between devices with their start and end apart: 8, of which 6 were waited for; matrix products, arithmetic and copies ran while one was open for 24% of the time, Pallas kernels for 0%

commit v1 on v0

--- a/solution.py
+++ b/solution.py
@@ -36,7 +36,7 @@
     picked_p = probs.reshape(-1)[flat_index].reshape(groups, slots_per)
     send_p = jnp.where(filled, picked_p, jnp.zeros_like(picked_p))
     dy3 = upstream.reshape(tok_rows, model_width // lanes, lanes)
-    dy_z = lax.all_gather(dy3, "z", axis=0, tiled=True)
+    dy_z = jnp.concatenate(lax.all_to_all(jnp.stack([dy3] * lax.axis_size("z")), "z", 0, 0), axis=0)
     dy_pair = lax.ppermute(dy_z, "core", perm=[(c, (c + 1) % n_core) for c in range(n_core)])
     dy_all = jnp.concatenate([dy_z, dy_pair], axis=0)
     w_blocks = lax.all_to_all(

time: 390 us -> 486 us (1.25)
  blocking collectives: 0 us -> 193 us
  waiting for transfers between devices: 234 us -> 136 us
    all_to_all x0 -> x1, blocking collectives: none -> 193 us  [body(): lax.all_to_all(jnp.stack([dy3] * lax.axis_size('z')), 'z', 0, 0)]
    all_gather x1 -> x0, waiting for transfers between devices: 98.1 us -> none  [body(): dy_z = lax.all_gather(dy3, 'z', axis=0, tiled=True)]
  transfers between devices with their start and end apart: 8 -> 7, of which waited for: 6 -> 5; matrix products, arithmetic and copies ran while one was open for 24% -> 19% of each run, Pallas kernels for 0% -> 0%
where the time goes in v1:
time: 486 us; the launch traced here: 485 us
  blocking collectives  193 us (40%)
  waiting for transfers between devices  136 us (28%)
  local copies, waits for them, and re-layouts  60.7 us (12%)
  starting transfers between devices  28.6 us (6%)
  matrix products  28.2 us (6%)
  other arithmetic  23.3 us (5%)
  between operations  14.3 us (3%)
    all_to_all x1, blocking collectives, body(): lax.all_to_all(jnp.stack([dy3] * lax.axis_size('z')), 'z', 0, 0)  193 us
    all_to_all x1, waiting for transfers between devices, body(): lax.all_to_all(jnp.broadcast_to(w_down, (n_dp,) + w_down.shape[1:]), 'dp'...  107 us
    gather x2, local copies, waits for them, and re-layouts, body(): rows_dy = dy_all[row_of.reshape(-1)]  24.7 us
    concatenate x1, other arithmetic, body(): dy_all = jnp.concatenate([dy_z, dy_pair], axis=0)  16.7 us
    dot_general x1, matrix products, body(): lax.dot_general(rows_h, w_full, (((1,), (2,)), ((), ())), preferred_eleme...  14.2 us
    reduce_scatter x1, waiting for transfers between devices, body(): lax.psum_scatter(partial.reshape(model_width, hid_width), 'dp', scatter_d...  14.1 us
    dot_general x1, matrix products, body(): lax.dot_general(scaled, rows_h, (((0,), (0,)), ((), ())), preferred_eleme...  14 us
  transfers between devices with their start and end apart: 7, of which 5 were waited for; matrix products, arithmetic and copies ran while one was open for 19% of the time, Pallas kernels for 0%

profile of v1, /device:TPU:1, one launch (start us, length us, event | category | flops | bytes accessed | tf_op | source)
XLA Modules:
  0.0 484.6 jit_solution(4995638491623192618)
XLA Ops:
  7.2 1.6 copy.58
  10.2 193.4 %all_to_all.45 = bf16[8,128,32,128]{3,2,1,0:T(8,128)(2,1)} all-to-all(bf16[8,128,32,128]{3,2,1,0:T(8,128)(2,1)S(1)} %stack.3), channel_id=1, replica_groups=mesh['dp'=16,'z'=8,'core'=2] {'z'}, dimensions={0} | all-to-all | bytes 16777216 | tf_op jit(solution)/shard_map/all_to_all | solution.py:39
  203.7 2.5 collective-permute-start
  209.1 7.3 %gather_fusion = bf16[1152]{0:T(1024)(128)(2,1)S(1)} fusion(bf16[1024]{0:T(1024)(128)(2,1)S(1)} %reshape.190, s32[2048]{0:T(1024)S(1)} %pad_clamp_fusion.1), kind=kCustom, calls=%fused_computation | custom fusion | bytes 9216 | tf_op jit(solution)/shard_map/gather | solution.py:36
  217.1 3.3 all-to-all-start
  220.4 4.6 gather_fusion.2
  224.9 2.5 all-to-all-done
  227.4 4.8 all-to-all-start.2
  233.6 5.5 %all-to-all-done.2 = s32[16,1,72]{2,1,0:T(1,128)S(1)} async-done(((s32[16,1,72]{2,1,0:T(1,128)}), s32[16,1,72]{2,1,0:T(1,128)S(1)}, u32[]{:S(2)}, u32[]{:S(2)}) %all-to-all-start.2) | async-done | bytes 4640 | tf_op jit(solution)/shard_map/all_to_all | solution.py:54
  239.2 4.2 all-to-all-start.3
  245.0 16.7 %pad_maximum_fusion = bf16[2048,32,128]{2,1,0:T(8,128)(2,1)} fusion(bf16[1024,32,128]{2,1,0:T(8,128)(2,1)} %collective-permute-done, bf16[1024,32,128]{2,1,0:T(8,128)(2,1)} %bitcast.1), kind=kLoop, calls=%fused_computation.8 | loop fusion | flops 8388608 | bytes 33554432 | tf_op jit(solution)/shard_map/concatenate | solution.py:41
  261.7 11.8 %gather_fusion.1 = bf16[1152,32,128]{2,1,0:T(8,128)(2,1)} fusion(bf16[2048,32,128]{2,1,0:T(8,128)(2,1)} %pad_maximum_fusion, s32[2048]{0:T(1024)S(1)} %pad_clamp_fusion), kind=kCustom, calls=%fused_computation.1 | custom fusion | bytes 18878976 | tf_op jit(solution)/shard_map/gather | solution.py:62
  273.5 12.9 %copy.53 = bf16[1152,32,128]{0,2,1:T(8,128)(2,1)} copy(bf16[1152,32,128]{2,1,0:T(8,128)(2,1)} %gather_fusion.1) | data formatting | bytes 18874368 | tf_op jit(solution)/shard_map/gather | solution.py:62
  286.4 14.0 %fusion.5 = bf16[32,128,768]{2,1,0:T(8,128)(2,1)} fusion(bf16[1152,768,1]{1,0,2:T(8,128)(2,1)S(1)} %bitcast.32, bf16[1152,32,128]{0,2,1:T(8,128)(2,1)} %copy.53, f32[1152]{0:T(1024)S(1)} %reshape.198), kind=kOutput, calls=%fused_computation.12 | convolution fusion | flops 7265058816 | bytes 17502720 | tf_op jit(solution)/shard_map/dot_general | solution.py:73
  300.4 3.3 broadcast_in_dim.54
  303.7 6.8 %all-to-all-start.4 = ((bf16[16,256,768]{2,1,0:T(8,128)(2,1)}), bf16[16,256,768]{2,1,0:T(8,128)(2,1)}, u32[]{:S(2)}, u32[]{:S(2)}) async-start(bf16[16,256,768]{2,1,0:T(8,128)(2,1)} %broadcast_in_dim.54), calls=%async_computation.5 | async-start | bytes 12582912 | tf_op jit(solution)/shard_map/all_to_all | solution.py:42
  310.8 7.1 %gather_fusion.4 = s32[1024]{0:T(1024)S(1)} fusion(s32[128,16]{1,0:T(8,128)S(1)} %broadcast_add_fusion, s32[1024]{0:T(1024)S(1)} %reshape.230), kind=kCustom, calls=%fused_computation.4 | custom fusion | bytes 16384 | tf_op jit(solution)/shard_map/jit(take_along_axis)/gather | solution.py:79
  318.0 107.3 %all-to-all-done.4 = bf16[16,256,768]{2,1,0:T(8,128)(2,1)} async-done(((bf16[16,256,768]{2,1,0:T(8,128)(2,1)}), bf16[16,256,768]{2,1,0:T(8,128)(2,1)}, u32[]{:S(2)}, u32[]{:S(2)}) %all-to-all-start.4) | async-done | bytes 6291488 | tf_op jit(solution)/shard_map/all_to_all | solution.py:42
  425.3 14.2 %fusion.4 = f32[1152]{0:T(1024)S(1)} fusion(bf16[1152,32,128]{0,2,1:T(8,128)(2,1)} %copy.53, bf16[1152,768,1]{1,0,2:T(8,128)(2,1)S(1)} %bitcast.33, bf16[32,128,768]{2,1,0:T(8,128)(2,1)} %bitcast.12), kind=kOutput, calls=%fused_computation.11 | convolution fusion | flops 7261912064 | bytes 17502720 | tf_op jit(solution)/shard_map/dot_general | solution.py:63
  440.2 7.1 %all-to-all-start.5 = ((f32[16,1,72]{2,1,0:T(1,128)}), f32[16,1,72]{2,1,0:T(1,128)S(1)}, u32[]{:S(2)}, u32[]{:S(2)}) async-start(f32[16,1,72]{2,1,0:T(1,128)} %all_to_all.36), calls=%async_computation.6 | async-start | bytes 16384 | tf_op jit(solution)/shard_map/all_to_all | solution.py:67
  447.4 6.7 %all-to-all-done.5 = f32[16,1,72]{2,1,0:T(1,128)S(1)} async-done(((f32[16,1,72]{2,1,0:T(1,128)}), f32[16,1,72]{2,1,0:T(1,128)S(1)}, u32[]{:S(2)}, u32[]{:S(2)}) %all-to-all-start.5) | async-done | bytes 4640 | tf_op jit(solution)/shard_map/all_to_all | solution.py:67
  454.2 6.8 %gather_fusion.3 = f32[1024]{0:T(1024)S(1)} fusion(f32[16,72]{1,0:T(8,128)S(1)} %bitcast.28, s32[1024]{0:T(1024)S(1)} %reshape.224), kind=kCustom, calls=%fused_computation.3 | custom fusion | bytes 16384 | tf_op jit(solution)/shard_map/gather | solution.py:80
  461.7 14.1 %reduce-scatter.2.cloned.1.call-done = bf16[256,768]{1,0:T(8,128)(2,1)} async-done(((bf16[4096,768]{1,0:T(8,128)(2,1)}), bf16[256,768]{1,0:T(8,128)(2,1)}) %reduce-scatter.2.cloned.1.call-update) | async-done | bytes 393232 | tf_op jit(solution)/shard_map/reduce_scatter | solution.py:76
  475.9 1.9 bitcast_convert_fusion
  (53 shorter events, 10.1 us)
Async XLA Ops:
  7.2 213.2 %copy-start = (bf16[128,8,768]{2,1,0:T(8,128)(2,1)S(1)}, bf16[128,8,768]{2,1,0:T(8,128)(2,1)}, u32[]{:S(2)}) copy-start(bf16[128,8,768]{2,1,0:T(8,128)(2,1)} %param.5) | copy-start | bytes 4718596
  10.2 195.9 %copy-start.3 = (s32[128,8]{0,1:T(8,128)S(1)}, s32[128,8]{0,1:T(8,128)}, u32[]{:S(2)}) copy-start(s32[128,8]{0,1:T(8,128)} %param.8) | copy-start | bytes 12292
  10.2 198.6 %copy-start.4 = (bf16[128,8]{0,1:T(8,128)(2,1)S(1)}, bf16[128,8]{0,1:T(8,128)(2,1)}, u32[]{:S(2)}) copy-start(bf16[128,8]{0,1:T(8,128)(2,1)} %param.7) | copy-start | bytes 6148
  203.7 41.3 %collective-permute-start = (bf16[1024,32,128]{2,1,0:T(8,128)(2,1)}, bf16[1024,32,128]{2,1,0:T(8,128)(2,1)}, u32[]{:S(2)}, u32[]{:S(2)}) collective-permute-start(bf16[1024,32,128]{2,1,0:T(8,128)(2,1)} %bitcast.1), channel_id=1, source_target_pairs={{0,1},{1,0},{2,3},{3,2},{4,5},{5,4},{6,7},{7,6},{8,9},{9,8},{10,11... | collective-permute-start | bytes 25165832 | tf_op jit(solution)/shard_map/ppermute | solution.py:40
  217.1 10.3 %all-to-all-start = ((bf16[16,1,72]{2,1,0:T(2,128)(2,1)}), bf16[16,1,72]{2,1,0:T(2,128)(2,1)S(1)}, u32[]{:S(2)}, u32[]{:S(2)}) async-start(bf16[16,1,72]{2,1,0:T(2,128)(2,1)} %copy.51), calls=%async_computation | async-start | bytes 16384 | tf_op jit(solution)/shard_map/all_to_all | solution.py:53
  227.4 11.7 %all-to-all-start.2 = ((s32[16,1,72]{2,1,0:T(1,128)}), s32[16,1,72]{2,1,0:T(1,128)S(1)}, u32[]{:S(2)}, u32[]{:S(2)}) async-start(s32[16,1,72]{2,1,0:T(1,128)} %bitcast.3), calls=%async_computation.2 | async-start | bytes 16384 | tf_op jit(solution)/shard_map/all_to_all | solution.py:54
  239.2 47.3 %all-to-all-start.3 = ((bf16[16,72,768]{2,1,0:T(8,128)(2,1)}), bf16[16,72,768]{2,1,0:T(8,128)(2,1)S(1)}, u32[]{:S(2)}, u32[]{:S(2)}) async-start(bf16[16,72,768]{2,1,0:T(8,128)(2,1)} %broadcast_select_fusion), calls=%async_computation.3 | async-start | bytes 3538944 | tf_op jit(solution)/shard_map/all_to_all | solution.py:52
  243.3 232.5 %reduce-scatter.2.cloned.1.call-start = ((), (), s32[]{:S(2)}) async-start(), calls=%async_computation.7 | async-start | bytes 6684672 | tf_op jit(solution)/shard_map/reduce_scatter | solution.py:76
  286.4 14.0 %copy-start.2 = (bf16[1,256,768]{2,1,0:T(8,128)(2,1)S(1)}, bf16[1,256,768]{2,1,0:T(8,128)(2,1)}, u32[]{:S(2)}) copy-start(bf16[1,256,768]{2,1,0:T(8,128)(2,1)} %param.9) | copy-start | bytes 1179652
  303.7 121.5 %all-to-all-start.4 = ((bf16[16,256,768]{2,1,0:T(8,128)(2,1)}), bf16[16,256,768]{2,1,0:T(8,128)(2,1)}, u32[]{:S(2)}, u32[]{:S(2)}) async-start(bf16[16,256,768]{2,1,0:T(8,128)(2,1)} %broadcast_in_dim.54), calls=%async_computation.5 | async-start | bytes 12582912 | tf_op jit(solution)/shard_map/all_to_all | solution.py:42
  440.2 14.0 %all-to-all-start.5 = ((f32[16,1,72]{2,1,0:T(1,128)}), f32[16,1,72]{2,1,0:T(1,128)S(1)}, u32[]{:S(2)}, u32[]{:S(2)}) async-start(f32[16,1,72]{2,1,0:T(1,128)} %all_to_all.36), calls=%async_computation.6 | async-start | bytes 16384 | tf_op jit(solution)/shard_map/all_to_all | solution.py:67
  454.2 23.6 %copy-start.1 = (bf16[128,8,768]{2,1,0:T(8,128)(2,1)S(1)}, bf16[128,8,768]{2,1,0:T(8,128)(2,1)}, u32[]{:S(2)}) copy-start(bf16[128,8,768]{2,1,0:T(8,128)(2,1)} %param.5) | copy-start | bytes 4718596
Sparse Core Ops, SparseCore 0:
  300.5 175.2 reduce-scatter.1
